TPU v7x, 512 devices: a whole 4x8x8 slice. The times are simulated.
512 devices in a mesh: param: 32 (over x, z), ex: 16 (over y, core).
Axes of the slice: x: 4, y: 8, z: 8, core: 2. Of those that a mesh axis runs over, the one named last changes fastest.
Arguments:
- adapter_gradients: bfloat16 [512, 131072], P('ex', 'param'), may hold values from -560 to 560
- sign_hash_keys: int32 [4], replicated, may hold values from 1 to 16777215
- target_indices: int32 [256], replicated, may hold values from 0 to 511
Outputs:
- features: float32 [512, 8192], P('ex', 'param')
- scores: float32 [512, 256], P('ex')
All inputs are finite; a program needn't handle non-finite values.
Results may differ from a plain program's by a relative error of at most 0.0003.
Values sent between devices are 32-bit elements; how exact they have to be, the bound alone decides.
No kernel may reach another device: no remote copies, remote signals or barrier semaphores. Data moves between devices by JAX's collectives and lax.ppermute only.
A program may use at most 128 MiB of HBM per device.

v0:
```python
import jax
import jax.numpy as jnp
from jax import lax
from jax.sharding import PartitionSpec as P

K = 8192
norm_eps = 1e-06


def sign_block(sign_hash_keys, first_row, row_count, col_count):
    mult_row = sign_hash_keys[0] | 1
    mult_col = sign_hash_keys[1] | 1
    seed_add = sign_hash_keys[2]
    mix_mult = sign_hash_keys[3] | 1
    row_ids = first_row + lax.iota(jnp.int32, row_count)[:, None]
    col_ids = lax.iota(jnp.int32, col_count)[None, :]
    hashed = row_ids * mult_row + col_ids * mult_col + seed_add
    hashed = hashed ^ lax.shift_right_logical(hashed, jnp.full_like(hashed, 16))
    hashed = hashed * mix_mult
    hashed = hashed ^ lax.shift_right_logical(hashed, jnp.full_like(hashed, 13))
    hashed = hashed * jnp.int32(-1028477387)
    hashed = hashed ^ lax.shift_right_logical(hashed, jnp.full_like(hashed, 16))
    return jnp.where(hashed < 0, 1.0, -1.0).astype(jnp.bfloat16)


def local(adapter_gradients, sign_hash_keys, target_indices):
    resident_example, resident_rows = adapter_gradients.shape
    row_base = lax.axis_index("param") * jnp.int32(resident_rows)
    turn_count = 8
    rows_per_tile = resident_rows // turn_count
    scale_k = jnp.float32(K)

    def accumulate(tile_idx, totals):
        start_offset = tile_idx * jnp.int32(rows_per_tile)
        gradient_slab = lax.dynamic_slice_in_dim(adapter_gradients, start_offset, rows_per_tile, 1)
        signs = sign_block(sign_hash_keys, row_base + start_offset, rows_per_tile, K)
        return totals + jnp.dot(gradient_slab, signs, preferred_element_type=jnp.float32)

    partial_sums = lax.fori_loop(
        jnp.int32(0),
        jnp.int32(turn_count),
        accumulate,
        jnp.zeros((resident_example, K), jnp.float32),
    )
    projected = lax.psum_scatter(partial_sums, "param", scatter_dimension=1, tiled=True)
    own_squares = jnp.sum(projected * projected, axis=1)
    total_sq = lax.psum(own_squares, "param")
    features = projected * jnp.sqrt(scale_k / (total_sq + norm_eps))[:, None]
    pool_rows = lax.all_gather(features, "ex", axis=0, tiled=True)
    targets = jnp.take(pool_rows, target_indices, axis=0)
    partial_dots = jnp.dot(features, targets.T, precision=lax.Precision.HIGHEST)
    scores = lax.psum(partial_dots, "param") / scale_k
    return (features, scores)


def solution(mesh):
    return jax.shard_map(
        local,
        mesh=mesh,
        in_specs=(P("ex", "param"), P(), P()),
        out_specs=(P("ex", "param"), P("ex", None)),
        check_vma=False,
    )
```

profile of v0, /device:TPU:8, one launch (start us, length us, event | category | flops | bytes accessed | tf_op | source)
XLA Modules:
  0.0 555.2 jit_solution(16775991105922428957)
XLA Ops:
  7.2 0.0 reduce-scatter.2.cloned.1.call-start
  7.2 1.4 fusion.24
  10.4 81.0 %while.12 = (s32[]{:T(128)}, f32[32,8192]{1,0:T(8,128)S(1)}, bf16[32,4096]{1,0:T(8,128)(2,1)}, s32[]{:T(128)}, s32[]{:T(128)}, /*index=5*/s32[]{:T(128)}, s32[4]...) while((s32[]{:T(128)}, f32[32,8192]{1,0:T(8,128)S(1)}, ...), condition=%wide.region_1.2_spmd.clone, body=%wide.region_0.1_spmd.clone.sunk | while | flops 323494912 | bytes 2200785 | solution.py:39
  10.5 1.3 slice.29
  11.8 8.8 %convolution_add_fusion.2 = f32[32,8192]{1,0:T(8,128)S(1)} fusion(s32[]{:T(128)} %get-tuple-element.187, s32[]{:T(128)} %bitcast.6, s32[8192]{0:T(1024)S(1)} %iota_multiply_fusion.2, s32[512]{0:T(512)S(1)} %add_multiply_fusion.2, f32[32,8192]{1,0:T(8,128)S(1)} %get-tuple-element.169, pred[]{:T(512)S(6)} %compare.3, ...), kind=kOutput, calls=%fused_computation.8.clone.1 | convolution fusion | flops 323485696 | bytes 2165765 | tf_op jit(solution)/shard_map/while/body/dot_general | solution.py:37
  20.6 1.3 slice.29
  21.9 8.8 %convolution_add_fusion.2 = f32[32,8192]{1,0:T(8,128)S(1)} fusion(s32[]{:T(128)} %get-tuple-element.187, s32[]{:T(128)} %bitcast.6, s32[8192]{0:T(1024)S(1)} %iota_multiply_fusion.2, s32[512]{0:T(512)S(1)} %add_multiply_fusion.2, f32[32,8192]{1,0:T(8,128)S(1)} %get-tuple-element.169, pred[]{:T(512)S(6)} %compare.3, ...), kind=kOutput, calls=%fused_computation.8.clone.1 | convolution fusion | flops 323485696 | bytes 2165765 | tf_op jit(solution)/shard_map/while/body/dot_general | solution.py:37
  30.8 1.3 slice.29
  32.1 8.8 %convolution_add_fusion.2 = f32[32,8192]{1,0:T(8,128)S(1)} fusion(s32[]{:T(128)} %get-tuple-element.187, s32[]{:T(128)} %bitcast.6, s32[8192]{0:T(1024)S(1)} %iota_multiply_fusion.2, s32[512]{0:T(512)S(1)} %add_multiply_fusion.2, f32[32,8192]{1,0:T(8,128)S(1)} %get-tuple-element.169, pred[]{:T(512)S(6)} %compare.3, ...), kind=kOutput, calls=%fused_computation.8.clone.1 | convolution fusion | flops 323485696 | bytes 2165765 | tf_op jit(solution)/shard_map/while/body/dot_general | solution.py:37
  40.9 1.3 slice.29
  42.2 8.8 %convolution_add_fusion.2 = f32[32,8192]{1,0:T(8,128)S(1)} fusion(s32[]{:T(128)} %get-tuple-element.187, s32[]{:T(128)} %bitcast.6, s32[8192]{0:T(1024)S(1)} %iota_multiply_fusion.2, s32[512]{0:T(512)S(1)} %add_multiply_fusion.2, f32[32,8192]{1,0:T(8,128)S(1)} %get-tuple-element.169, pred[]{:T(512)S(6)} %compare.3, ...), kind=kOutput, calls=%fused_computation.8.clone.1 | convolution fusion | flops 323485696 | bytes 2165765 | tf_op jit(solution)/shard_map/while/body/dot_general | solution.py:37
  51.0 1.3 slice.29
  52.3 8.8 %convolution_add_fusion.2 = f32[32,8192]{1,0:T(8,128)S(1)} fusion(s32[]{:T(128)} %get-tuple-element.187, s32[]{:T(128)} %bitcast.6, s32[8192]{0:T(1024)S(1)} %iota_multiply_fusion.2, s32[512]{0:T(512)S(1)} %add_multiply_fusion.2, f32[32,8192]{1,0:T(8,128)S(1)} %get-tuple-element.169, pred[]{:T(512)S(6)} %compare.3, ...), kind=kOutput, calls=%fused_computation.8.clone.1 | convolution fusion | flops 323485696 | bytes 2165765 | tf_op jit(solution)/shard_map/while/body/dot_general | solution.py:37
  61.1 1.3 slice.29
  62.4 8.8 %convolution_add_fusion.2 = f32[32,8192]{1,0:T(8,128)S(1)} fusion(s32[]{:T(128)} %get-tuple-element.187, s32[]{:T(128)} %bitcast.6, s32[8192]{0:T(1024)S(1)} %iota_multiply_fusion.2, s32[512]{0:T(512)S(1)} %add_multiply_fusion.2, f32[32,8192]{1,0:T(8,128)S(1)} %get-tuple-element.169, pred[]{:T(512)S(6)} %compare.3, ...), kind=kOutput, calls=%fused_computation.8.clone.1 | convolution fusion | flops 323485696 | bytes 2165765 | tf_op jit(solution)/shard_map/while/body/dot_general | solution.py:37
  71.3 1.3 slice.29
  72.6 8.8 %convolution_add_fusion.2 = f32[32,8192]{1,0:T(8,128)S(1)} fusion(s32[]{:T(128)} %get-tuple-element.187, s32[]{:T(128)} %bitcast.6, s32[8192]{0:T(1024)S(1)} %iota_multiply_fusion.2, s32[512]{0:T(512)S(1)} %add_multiply_fusion.2, f32[32,8192]{1,0:T(8,128)S(1)} %get-tuple-element.169, pred[]{:T(512)S(6)} %compare.3, ...), kind=kOutput, calls=%fused_computation.8.clone.1 | convolution fusion | flops 323485696 | bytes 2165765 | tf_op jit(solution)/shard_map/while/body/dot_general | solution.py:37
  81.4 1.3 slice.29
  82.7 8.8 %convolution_add_fusion.2 = f32[32,8192]{1,0:T(8,128)S(1)} fusion(s32[]{:T(128)} %get-tuple-element.187, s32[]{:T(128)} %bitcast.6, s32[8192]{0:T(1024)S(1)} %iota_multiply_fusion.2, s32[512]{0:T(512)S(1)} %add_multiply_fusion.2, f32[32,8192]{1,0:T(8,128)S(1)} %get-tuple-element.169, pred[]{:T(512)S(6)} %compare.3, ...), kind=kOutput, calls=%fused_computation.8.clone.1 | convolution fusion | flops 323485696 | bytes 2165765 | tf_op jit(solution)/shard_map/while/body/dot_general | solution.py:37
  91.5 0.0 copy-start.2
  91.5 1.0 copy-done
  92.5 0.0 reduce-scatter.2.cloned.1.call-update
  92.5 225.0 %reduce-scatter.2.cloned.1.call-done = f32[32,256]{1,0:T(8,128)} async-done(((f32[32,8192]{1,0:T(8,128)}), f32[32,256]{1,0:T(8,128)}) %reduce-scatter.2.cloned.1.call-update) | async-done | bytes 32784 | tf_op jit(solution)/shard_map/reduce_scatter | solution.py:45
  317.6 0.9 multiply_reduce_fusion
  318.4 72.3 %psum.14 = f32[32]{0:T(128)S(1)} all-reduce(f32[32]{0:T(128)S(1)} %multiply_reduce_fusion), channel_id=1, replica_groups=mesh['param'=32,'ex'=16] {'param'}, use_global_device_ids=true, to_apply=%region_4.5 | all-reduce | flops 32 | bytes 256 | tf_op jit(solution)/shard_map/psum | solution.py:47
  390.7 0.8 broadcast_multiply_fusion.1
  391.5 17.1 %all_gather.3 = f32[512,256]{1,0:T(8,128)S(1)} all-gather(f32[32,256]{1,0:T(8,128)S(1)} %broadcast_multiply_fusion.1), channel_id=1, replica_groups=mesh['param'=32,'ex'=16] {'ex'}, dimensions={0}, use_global_device_ids=true | all-gather | bytes 557056 | tf_op jit(solution)/shard_map/all_gather | solution.py:49
  408.7 1.0 gather_fusion
  409.6 0.0 copy-done.1
  409.6 0.4 fusion.19
  410.1 137.7 %psum.15 = f32[32,256]{1,0:T(8,128)S(1)} all-reduce(f32[32,256]{1,0:T(8,128)S(1)} %fusion.19), channel_id=1, replica_groups=mesh['param'=32,'ex'=16] {'param'}, use_global_device_ids=true, to_apply=%region_5.6 | all-reduce | flops 8192 | bytes 65536 | tf_op jit(solution)/shard_map/psum | solution.py:52
  547.7 0.6 broadcast_multiply_fusion
  (24 shorter events, 0.2 us)
Async XLA Ops:
  7.2 310.4 %reduce-scatter.2.cloned.1.call-start = ((), (), s32[]{:S(2)}) async-start(), calls=%async_computation.1 | async-start | bytes 1081344 | tf_op jit(solution)/shard_map/reduce_scatter | solution.py:45
  91.5 1.0 copy-start
  91.5 1.0 copy-start.2
  391.5 18.1 %copy-start.1 = (f32[32,256]{1,0:T(8,128)}, f32[32,256]{1,0:T(8,128)S(1)}, u32[]{:S(2)}) copy-start(f32[32,256]{1,0:T(8,128)S(1)} %broadcast_multiply_fusion.1) | copy-start | bytes 98308
Sparse Core Ops, SparseCore 0:
  92.6 224.9 reduce-scatter.1
where the time goes:
time: 556 us; the launch traced here: 555 us
  blocking collectives  227 us (41%)
  waiting for transfers between devices  225 us (40%)
  matrix products  70.5 us (13%)
  between operations  16 us (3%)
  local copies, waits for them, and re-layouts  13.7 us (2%)
    reduce_scatter x1, waiting for transfers between devices, local(): lax.psum_scatter(partial_sums, 'param', scatter_dimension=1, tiled=True)  225 us
    psum x1, blocking collectives, local(): scores = lax.psum(partial_dots, 'param') / scale_k  138 us
    psum x1, blocking collectives, local(): total_sq = lax.psum(own_squares, 'param')  72.3 us
    dot_general x8, matrix products, accumulate(): jnp.dot(gradient_slab, signs, preferred_element_type=jnp.float32)  70 us
    all_gather x1, blocking collectives, local(): pool_rows = lax.all_gather(features, 'ex', axis=0, tiled=True)  17.1 us
  transfers between devices with their start and end apart: 1, of which 1 were waited for; matrix products, arithmetic and copies ran while one was open for 0% of the time, Pallas kernels for 0%

commit v1 on v0

--- a/solution.py
+++ b/solution.py
@@ -46,7 +46,12 @@
     own_squares = jnp.sum(projected * projected, axis=1)
     total_sq = lax.psum(own_squares, "param")
     features = projected * jnp.sqrt(scale_k / (total_sq + norm_eps))[:, None]
-    pool_rows = lax.all_gather(features, "ex", axis=0, tiled=True)
+    ring = [features]
+    for hop in range(15):
+        ring.append(lax.ppermute(ring[-1], "ex", [(dev, (dev + 1) % 16) for dev in range(16)]))
+    pool_rows = jnp.roll(
+        jnp.concatenate(ring[::-1], axis=0), (lax.axis_index("ex") + 1) * ring[0].shape[0], axis=0
+    )
     targets = jnp.take(pool_rows, target_indices, axis=0)
     partial_dots = jnp.dot(features, targets.T, precision=lax.Precision.HIGHEST)
     scores = lax.psum(partial_dots, "param") / scale_k

time: 556 us -> 608 us (1.094)
  the two profiles are of different devices: /device:TPU:8 before, /device:TPU:32 now
where the time goes in v1:
time: 608 us; the launch traced here: 607 us
  waiting for transfers between devices  293 us (48%)
  blocking collectives  210 us (35%)
  matrix products  70.4 us (12%)
  between operations  16.2 us (3%)
  local copies, waits for them, and re-layouts  13.9 us (2%)
    reduce_scatter x1, waiting for transfers between devices, local(): lax.psum_scatter(partial_sums, 'param', scatter_dimension=1, tiled=True)  225 us
    psum x1, blocking collectives, local(): scores = lax.psum(partial_dots, 'param') / scale_k  138 us
    psum x1, blocking collectives, local(): total_sq = lax.psum(own_squares, 'param')  72.2 us
    dot_general x8, matrix products, accumulate(): jnp.dot(gradient_slab, signs, preferred_element_type=jnp.float32)  70 us
    ppermute x15, waiting for transfers between devices, local(): lax.ppermute(ring[-1], 'ex', [(dev, (dev + 1) % 16) for dev in range(16)])  68.2 us
  transfers between devices with their start and end apart: 16, of which 16 were waited for; matrix products, arithmetic and copies ran while one was open for 0% of the time, Pallas kernels for 0%

profile of v1, /device:TPU:32, one launch (start us, length us, event | category | flops | bytes accessed | tf_op | source)
XLA Modules:
  0.0 606.6 jit_solution(7384862253227043903)
XLA Ops:
  7.2 1.4 fusion.24
  10.4 80.9 %while.12 = (s32[]{:T(128)}, f32[32,8192]{1,0:T(8,128)S(1)}, bf16[32,4096]{1,0:T(8,128)(2,1)}, s32[]{:T(128)}, s32[]{:T(128)}, /*index=5*/s32[]{:T(128)}, s32[4]...) while((s32[]{:T(128)}, f32[32,8192]{1,0:T(8,128)S(1)}, ...), condition=%wide.region_1.2_spmd.clone, body=%wide.region_0.1_spmd.clone.sunk | while | flops 323494912 | bytes 2200785 | solution.py:39
  10.5 1.3 slice.29
  11.8 8.7 %convolution_add_fusion.2 = f32[32,8192]{1,0:T(8,128)S(1)} fusion(s32[]{:T(128)} %get-tuple-element.187, s32[]{:T(128)} %bitcast.6, s32[8192]{0:T(1024)S(1)} %iota_multiply_fusion.2, s32[512]{0:T(512)S(1)} %add_multiply_fusion.2, f32[32,8192]{1,0:T(8,128)S(1)} %get-tuple-element.169, pred[]{:T(512)S(6)} %compare.4, ...), kind=kOutput, calls=%fused_computation.8.clone.1 | convolution fusion | flops 323485696 | bytes 2165765 | tf_op jit(solution)/shard_map/while/body/dot_general | solution.py:37
  20.6 1.3 slice.29
  21.9 8.7 %convolution_add_fusion.2 = f32[32,8192]{1,0:T(8,128)S(1)} fusion(s32[]{:T(128)} %get-tuple-element.187, s32[]{:T(128)} %bitcast.6, s32[8192]{0:T(1024)S(1)} %iota_multiply_fusion.2, s32[512]{0:T(512)S(1)} %add_multiply_fusion.2, f32[32,8192]{1,0:T(8,128)S(1)} %get-tuple-element.169, pred[]{:T(512)S(6)} %compare.4, ...), kind=kOutput, calls=%fused_computation.8.clone.1 | convolution fusion | flops 323485696 | bytes 2165765 | tf_op jit(solution)/shard_map/while/body/dot_general | solution.py:37
  32.0 8.7 %convolution_add_fusion.2 = f32[32,8192]{1,0:T(8,128)S(1)} fusion(s32[]{:T(128)} %get-tuple-element.187, s32[]{:T(128)} %bitcast.6, s32[8192]{0:T(1024)S(1)} %iota_multiply_fusion.2, s32[512]{0:T(512)S(1)} %add_multiply_fusion.2, f32[32,8192]{1,0:T(8,128)S(1)} %get-tuple-element.169, pred[]{:T(512)S(6)} %compare.4, ...), kind=kOutput, calls=%fused_computation.8.clone.1 | convolution fusion | flops 323485696 | bytes 2165765 | tf_op jit(solution)/shard_map/while/body/dot_general | solution.py:37
  40.8 1.3 slice.29
  42.1 8.7 %convolution_add_fusion.2 = f32[32,8192]{1,0:T(8,128)S(1)} fusion(s32[]{:T(128)} %get-tuple-element.187, s32[]{:T(128)} %bitcast.6, s32[8192]{0:T(1024)S(1)} %iota_multiply_fusion.2, s32[512]{0:T(512)S(1)} %add_multiply_fusion.2, f32[32,8192]{1,0:T(8,128)S(1)} %get-tuple-element.169, pred[]{:T(512)S(6)} %compare.4, ...), kind=kOutput, calls=%fused_computation.8.clone.1 | convolution fusion | flops 323485696 | bytes 2165765 | tf_op jit(solution)/shard_map/while/body/dot_general | solution.py:37
  52.3 8.7 %convolution_add_fusion.2 = f32[32,8192]{1,0:T(8,128)S(1)} fusion(s32[]{:T(128)} %get-tuple-element.187, s32[]{:T(128)} %bitcast.6, s32[8192]{0:T(1024)S(1)} %iota_multiply_fusion.2, s32[512]{0:T(512)S(1)} %add_multiply_fusion.2, f32[32,8192]{1,0:T(8,128)S(1)} %get-tuple-element.169, pred[]{:T(512)S(6)} %compare.4, ...), kind=kOutput, calls=%fused_computation.8.clone.1 | convolution fusion | flops 323485696 | bytes 2165765 | tf_op jit(solution)/shard_map/while/body/dot_general | solution.py:37
  62.4 8.7 %convolution_add_fusion.2 = f32[32,8192]{1,0:T(8,128)S(1)} fusion(s32[]{:T(128)} %get-tuple-element.187, s32[]{:T(128)} %bitcast.6, s32[8192]{0:T(1024)S(1)} %iota_multiply_fusion.2, s32[512]{0:T(512)S(1)} %add_multiply_fusion.2, f32[32,8192]{1,0:T(8,128)S(1)} %get-tuple-element.169, pred[]{:T(512)S(6)} %compare.4, ...), kind=kOutput, calls=%fused_computation.8.clone.1 | convolution fusion | flops 323485696 | bytes 2165765 | tf_op jit(solution)/shard_map/while/body/dot_general | solution.py:37
  72.5 8.7 %convolution_add_fusion.2 = f32[32,8192]{1,0:T(8,128)S(1)} fusion(s32[]{:T(128)} %get-tuple-element.187, s32[]{:T(128)} %bitcast.6, s32[8192]{0:T(1024)S(1)} %iota_multiply_fusion.2, s32[512]{0:T(512)S(1)} %add_multiply_fusion.2, f32[32,8192]{1,0:T(8,128)S(1)} %get-tuple-element.169, pred[]{:T(512)S(6)} %compare.4, ...), kind=kOutput, calls=%fused_computation.8.clone.1 | convolution fusion | flops 323485696 | bytes 2165765 | tf_op jit(solution)/shard_map/while/body/dot_general | solution.py:37
  81.3 1.3 slice.29
  82.6 8.7 %convolution_add_fusion.2 = f32[32,8192]{1,0:T(8,128)S(1)} fusion(s32[]{:T(128)} %get-tuple-element.187, s32[]{:T(128)} %bitcast.6, s32[8192]{0:T(1024)S(1)} %iota_multiply_fusion.2, s32[512]{0:T(512)S(1)} %add_multiply_fusion.2, f32[32,8192]{1,0:T(8,128)S(1)} %get-tuple-element.169, pred[]{:T(512)S(6)} %compare.4, ...), kind=kOutput, calls=%fused_computation.8.clone.1 | convolution fusion | flops 323485696 | bytes 2165765 | tf_op jit(solution)/shard_map/while/body/dot_general | solution.py:37
  92.4 224.8 %reduce-scatter.2.cloned.1.call-done = f32[32,256]{1,0:T(8,128)} async-done(((f32[32,8192]{1,0:T(8,128)}), f32[32,256]{1,0:T(8,128)}) %reduce-scatter.2.cloned.1.call-update) | async-done | bytes 32784 | tf_op jit(solution)/shard_map/reduce_scatter | solution.py:45
  318.1 72.2 %psum.14 = f32[32]{0:T(128)S(1)} all-reduce(f32[32]{0:T(128)S(1)} %multiply_reduce_fusion), channel_id=1, replica_groups=mesh['param'=32,'ex'=16] {'param'}, use_global_device_ids=true, to_apply=%region_4.5 | all-reduce | flops 32 | bytes 256 | tf_op jit(solution)/shard_map/psum | solution.py:47
  391.2 4.5 collective-permute-done
  395.8 4.5 collective-permute-done.1
  400.3 4.5 collective-permute-done.2
  404.9 4.5 collective-permute-done.3
  409.4 4.5 collective-permute-done.4
  414.0 4.5 collective-permute-done.5
  418.5 4.5 collective-permute-done.6
  423.1 4.5 collective-permute-done.7
  427.6 4.5 collective-permute-done.8
  432.2 4.5 collective-permute-done.9
  436.7 4.5 collective-permute-done.10
  441.3 4.5 collective-permute-done.11
  445.9 4.5 collective-permute-done.12
  450.4 4.5 collective-permute-done.13
  455.0 4.5 collective-permute-done.14
  461.5 137.7 %psum.15 = f32[32,256]{1,0:T(8,128)S(1)} all-reduce(f32[32,256]{1,0:T(8,128)S(1)} %fusion.19), channel_id=1, replica_groups=mesh['param'=32,'ex'=16] {'param'}, use_global_device_ids=true, to_apply=%region_5.6 | all-reduce | flops 8192 | bytes 65536 | tf_op jit(solution)/shard_map/psum | solution.py:57
  (88 shorter events, 10.5 us)
Async XLA Ops:
  7.2 310.0 %reduce-scatter.2.cloned.1.call-start = ((), (), s32[]{:S(2)}) async-start(), calls=%async_computation.1 | async-start | bytes 1081344 | tf_op jit(solution)/shard_map/reduce_scatter | solution.py:45
  91.4 1.0 copy-start
  91.4 354.5 %copy-start.3 = (s32[256]{0:T(256)S(1)}, s32[256]{0:T(256)}, u32[]{:S(2)}) copy-start(s32[256]{0:T(256)} %param.7) | copy-start | bytes 3076
  317.2 142.5 %copy-start.1 = (f32[32,256]{1,0:T(8,128)S(1)}, f32[32,256]{1,0:T(8,128)}, u32[]{:S(2)}) copy-start(f32[32,256]{1,0:T(8,128)} %reduce-scatter.2.cloned.1.call-done) | copy-start | bytes 98308
  391.2 69.8 %copy-start.2 = (f32[32,256]{1,0:T(8,128)}, f32[32,256]{1,0:T(8,128)S(1)}, u32[]{:S(2)}) copy-start(f32[32,256]{1,0:T(8,128)S(1)} %broadcast_multiply_fusion.1) | copy-start | bytes 98308
  391.2 4.6 collective-permute-start
  395.8 4.6 collective-permute-start.1
  400.3 4.6 collective-permute-start.2
  404.9 4.6 collective-permute-start.3
  409.4 4.6 collective-permute-start.4
  414.0 4.6 collective-permute-start.5
  418.5 4.6 collective-permute-start.6
  423.1 4.6 collective-permute-start.7
  427.6 4.6 collective-permute-start.8
  432.2 4.6 collective-permute-start.9
  436.7 4.6 collective-permute-start.10
  441.3 4.6 collective-permute-start.11
  445.8 4.6 collective-permute-start.12
  450.4 4.6 collective-permute-start.13
  454.9 4.6 collective-permute-start.14
Sparse Core Ops, SparseCore 0:
  92.5 224.6 reduce-scatter.1
